TPU v7x, 32 devices: a whole 2x2x4 slice. The times are simulated.
32 devices in a mesh: gx: 8 (over y, x, core), gy: 4 (over z).
Axes of the slice: x: 2, y: 2, z: 4, core: 2. Of those that a mesh axis runs over, the one named last changes fastest.
Arguments:
- temp_start: float32 [8, 1024, 2048], P(None, ('gx', 'gy')), may hold values from -6 to 6
- heat_input: float32 [8, 1024, 2048], P(None, ('gx', 'gy')), may hold values from -3 to 3
- lateral: float32 [8], replicated, may hold values from 0.03 to 0.15
- vertical: float32 [7], replicated, may hold values from 0.03 to 0.15
- weighting: float32 [8], replicated, may hold values from -1 to 1
- modulus: float32 [1024, 2048], P('gx', 'gy'), may hold values from 0.3 to 3
- warp_prev: float32 [1024, 2048], P('gx', 'gy'), may hold values from -6 to 6
- joint_cell: int32 [65536], P(('gx', 'gy')), may hold values from 0 to 65535
- joint_owner: int32 [65536, 1], P(('gx', 'gy')), may hold values from 0 to 31; in each aligned block of 2048 rows (0 to 2047, 2048 to 4095, ...) at most 192 rows name the same one
- joint_strain: float32 [2, 32, 6144], P(None, ('gx', 'gy')), may hold values from -4 to 4
- joint_resist: float32 [32, 6144], P(('gx', 'gy')), may hold values from 1 to 2
Outputs:
- warpage: float32 [1024, 2048], P('gx', 'gy')
- strain_next: float32 [2, 32, 6144], P(None, ('gx', 'gy'))
- resist_next: float32 [32, 6144], P(('gx', 'gy'))
Inputs may be any that keep to these rules, and one draw needn't show every extreme that they name: `joint_owner`: among the 2048 joints of one device at most 192 have the same owner, and on some device exactly 192 do.
All inputs are finite; a program needn't handle non-finite values.
Results may differ from a plain program's by a relative error of at most 0.0003.
Values sent between devices are 32-bit elements; how exact they have to be, the bound alone decides.
No kernel may reach another device: no remote copies, remote signals or barrier semaphores. Data moves between devices by JAX's collectives and lax.ppermute only.
A program may use at most 320 MiB of HBM per device.

v0:
```python
import jax
import jax.numpy as jnp
from jax import lax
from jax.sharding import PartitionSpec as P

STEPS = 2
SWEEPS = 3
stiffness = 0.2
shear_mod = 0.6
rate_scale = 0.5
sat_level = 2.5
sat_power = 0.3
harden = 2.0
FLAT = ("gx", "gy")


def exchange(last, leading, axis):
    count = lax.axis_size(axis)
    up = [(i, i + 1) for i in range(count - 1)]
    down = [(j, i) for i, j in up]
    return (lax.ppermute(last, axis, up), lax.ppermute(leading, axis, down))


def with_halo(array, sides, width):
    for axis, dim in sides:
        length = array.shape[dim]
        last = lax.slice_in_dim(array, length - width, length, axis=dim)
        leading = lax.slice_in_dim(array, 0, width, axis=dim)
        before, after = exchange(last, leading, axis)
        array = jnp.concatenate([before, array, after], axis=dim)
    return array


def thermal_step(ext, heat_rows, lateral, vertical):
    cols = jnp.pad(ext, ((0, 0), (0, 0), (1, 1)))
    center = ext[:, 1:-1]
    lap = ext[:, 2:] + ext[:, :-2] + cols[:, 1:-1, 2:] + cols[:, 1:-1, :-2] - 4.0 * center
    flux = vertical[:, None, None] * (center[1:] - center[:-1])
    vert = jnp.pad(flux, ((0, 1), (0, 0), (0, 0))) - jnp.pad(flux, ((1, 0), (0, 0), (0, 0)))
    return center + lateral[:, None, None] * lap + vert + heat_rows


def moment_of(field, weighting):
    total = weighting[0] * field[0]
    for layer in range(1, field.shape[0]):
        total = total + weighting[layer] * field[layer]
    return total


def sweep(w_pad, e_pad, load):
    center = e_pad[1:-1, 1:-1]
    e_up = 0.5 * (center + e_pad[:-2, 1:-1])
    e_down = 0.5 * (center + e_pad[2:, 1:-1])
    e_left = 0.5 * (center + e_pad[1:-1, :-2])
    e_right = 0.5 * (center + e_pad[1:-1, 2:])
    numer = (
        load
        + e_up * w_pad[:-2, 1:-1]
        + e_down * w_pad[2:, 1:-1]
        + e_left * w_pad[1:-1, :-2]
        + e_right * w_pad[1:-1, 2:]
    )
    denom = stiffness + e_up + e_down + e_left + e_right
    return numer / denom


def anand(strain, resist, recv):
    total, inelastic = (strain[0], strain[1])
    increment, theta, live = (recv[0], recv[1], recv[2])
    total_new = total + increment
    arrhen = jnp.exp(2.0 - 2.0 / (1.0 + 0.1 * theta * theta))
    hyper = jnp.sinh(shear_mod * (total_new - inelastic) / resist)
    rate = rate_scale * arrhen * hyper * jnp.abs(hyper)
    inelastic_new = inelastic + rate
    target = sat_level * jnp.power(1.0 + jnp.abs(rate) / arrhen, sat_power)
    resist_new = resist + harden * (1.0 - resist / target) * jnp.abs(rate)
    keep = live > 0.5
    strain_out = jnp.stack(
        [jnp.where(keep, total_new, total), jnp.where(keep, inelastic_new, inelastic)]
    )
    return (strain_out, jnp.where(keep, resist_new, resist))


def thermal(temp, heat, lateral, vertical):
    devices = lax.axis_size(FLAT)
    t = lax.axis_index(FLAT)
    rows = temp.shape[1]
    h = STEPS
    last = jnp.concatenate([temp[:, rows - h :], heat[:, rows - (h - 1) :]], axis=1)
    leading = jnp.concatenate([temp[:, :h], heat[:, : h - 1]], axis=1)
    before, after = exchange(last, leading, FLAT)
    ext = jnp.concatenate([before[:, :h], temp, after[:, :h]], axis=1)
    heat_ext = jnp.concatenate([before[:, h:], heat, after[:, h:]], axis=1)
    for step in range(1, STEPS + 1):
        r = STEPS - step
        heat_rows = heat_ext[:, h - 1 - r : h - 1 - r + rows + 2 * r]
        ext = thermal_step(ext, heat_rows, lateral, vertical)
        if r > 0:
            g = t * rows + jnp.arange(-r, rows + r)
            inside = (g >= 0) & (g < devices * rows)
            ext = jnp.where(inside[None, :, None], ext, 0.0)
    return ext


def relay(load, top, width):
    n_gy = lax.axis_size("gy")
    rows, cols = load.shape
    cm = cols // n_gy
    before, after = exchange(load[rows - width :], load[:width], FLAT)
    load_ext = jnp.concatenate([before, load, after], axis=0)
    lp = jnp.pad(load_ext, ((0, 0), (width, width)))
    tp = jnp.pad(top, ((width, width), (width, width)))
    both = jnp.stack([lp, tp])
    send = jnp.stack([both[:, :, k * cm : k * cm + cm + 2 * width] for k in range(n_gy)])
    recv = lax.all_to_all(send, "gy", split_axis=0, concat_axis=0, tiled=True)
    parts = []
    for k in range(n_gy):
        lo = 0 if k == 0 else width
        hi = rows + 2 * width if k == n_gy - 1 else rows + width
        parts.append(recv[k, 0, lo:hi])
    load_m = jnp.concatenate(parts, axis=0)
    top_m = jnp.concatenate(
        [recv[k, 1, width : rows + width, width : cm + width] for k in range(n_gy)], axis=0
    )
    return (load_m, top_m)


def joint_ranks(owners, devices):
    count = owners.shape[0]
    block = 128 if count % 128 == 0 else count
    nb = count // block
    onehot = (owners[:, None] == jnp.arange(devices, dtype=jnp.int32)[None, :]).astype(jnp.float32)
    oh = onehot.reshape(nb, block, devices)
    ar = jnp.arange(block)
    tri = (ar[:, None] >= ar[None, :]).astype(jnp.float32)
    within = jnp.einsum("ij,bjd->bid", tri, oh, precision=lax.Precision.HIGHEST)
    totals = within[:, -1, :]
    ab = jnp.arange(nb)
    stri = (ab[:, None] > ab[None, :]).astype(jnp.float32)
    offs = jnp.dot(stri, totals, precision=lax.Precision.HIGHEST)
    cum = (within + offs[:, None, :]).reshape(count, devices)
    return jnp.sum(cum * onehot, axis=1).astype(jnp.int32) - 1


def body(
    temp_start,
    heat_input,
    lateral,
    vertical,
    weighting,
    modulus,
    warp_prev,
    joint_cell,
    joint_owner,
    joint_strain,
    joint_resist,
):
    devices = lax.axis_size(FLAT)
    n_gx, n_gy = (lax.axis_size("gx"), lax.axis_size("gy"))
    gi, gj = (lax.axis_index("gx"), lax.axis_index("gy"))
    rm, cm = warp_prev.shape
    wm = with_halo(jnp.stack([warp_prev, modulus]), (("gx", 1), ("gy", 2)), SWEEPS)
    owners = joint_owner[:, 0]
    capacity = joint_resist.shape[1] // devices
    slots = owners * capacity + joint_ranks(owners, devices)
    temp = thermal(temp_start, heat_input, lateral, vertical)
    load_t = moment_of(temp, weighting)
    load, top = relay(load_t, temp[-1], SWEEPS - 1)
    warp = wm[0]
    mod_ext = wm[1]
    for step in range(1, SWEEPS + 1):
        r = SWEEPS - step
        off = SWEEPS - (r + 1)
        e_pad = mod_ext[off : off + rm + 2 * r + 2, off : off + cm + 2 * r + 2]
        lo = SWEEPS - 1 - r
        ld = load[lo : lo + rm + 2 * r, lo : lo + cm + 2 * r]
        warp = sweep(warp, e_pad, ld)
        if r > 0:
            gr = gi * rm + jnp.arange(-r, rm + r)
            gc = gj * cm + jnp.arange(-r, cm + r)
            inside = ((gr >= 0) & (gr < n_gx * rm))[:, None] & ((gc >= 0) & (gc < n_gy * cm))[
                None, :
            ]
            warp = jnp.where(inside, warp, 0.0)
    fields = jnp.stack([(warp - warp_prev).reshape(-1), top.reshape(-1)])
    picked = fields[:, joint_cell]
    values = jnp.concatenate([picked, jnp.ones_like(picked[:1])], axis=0)
    outgoing = jnp.zeros((3, devices * capacity), jnp.float32).at[:, slots].set(values)
    incoming = lax.all_to_all(outgoing, FLAT, split_axis=1, concat_axis=1, tiled=True)
    strain_next, resist_next = anand(joint_strain, joint_resist, incoming[:, None, :])
    return (warp, strain_next, resist_next)


def solution(mesh):
    return jax.shard_map(
        body,
        mesh=mesh,
        in_specs=(
            P(None, FLAT, None),
            P(None, FLAT, None),
            P(),
            P(),
            P(),
            P("gx", "gy"),
            P("gx", "gy"),
            P(FLAT),
            P(FLAT, None),
            P(None, FLAT, None),
            P(FLAT, None),
        ),
        out_specs=(P("gx", "gy"), P(None, FLAT, None), P(FLAT, None)),
        check_vma=False,
    )
```

profile of v0, /device:TPU:0, one launch (start us, length us, event | category | flops | bytes accessed | tf_op | source)
XLA Modules:
  0.0 136.8 jit_solution(4110263155972718763)
XLA Ops:
  0.7 1.4 %fusion.88 = (f32[8,2,2048]{2,1,0:T(2,128)S(1)}, f32[8,2,2048]{2,1,0:T(2,128)S(1)}) fusion(f32[8,32,2048]{2,1,0:T(8,128)} %param.11), kind=kLoop, calls=%fused_computation.191 | loop fusion | bytes 524288 | tf_op jit(solution)/shard_map/slice | solution.py:89
  2.1 1.3 fusion.89
  3.5 5.0 %collective-permute-start = (f32[8,3,2048]{2,1,0:T(4,128)S(1)}, f32[8,3,2048]{2,1,0:T(4,128)S(1)}, u32[]{:S(2)}, u32[]{:S(2)}) collective-permute-start(f32[8,3,2048]{2,1,0:T(4,128)S(1)} %pad_maximum_fusion.5), channel_id=1, source_target_pairs={{0,1},{1,2},{2,3},{3,4},{4,5},{5,6},{6,7},{7,8},{8,9},{9,10},{10,1... | collective-permute-start | bytes 589832 | tf_op jit(solution)/shard_map/ppermute | solution.py:21
  8.6 1.3 collective-permute-start.1
  9.9 0.8 pad_maximum_fusion.14
  10.7 4.7 %collective-permute-start.4 = (f32[2,3,512]{2,1,0:T(4,128)S(1)}, f32[2,3,512]{2,1,0:T(4,128)S(1)}, u32[]{:S(2)}, u32[]{:S(2)}) collective-permute-start(f32[2,3,512]{2,1,0:T(4,128)S(1)} %get-tuple-element.31), channel_id=1, source_target_pairs={{0,4},{4,8},{8,12},{12,16},{16,20},{20,24},{24,28},{1,5},{5,9},{9,... | collective-permute-start | bytes 36872 | tf_op jit(solution)/shard_map/ppermute | solution.py:21
  15.4 1.3 collective-permute-start.5
  16.7 1.6 %fusion.94 = (f32[1]{0:T(128)}, f32[1]{0:T(128)}, f32[1]{0:T(128)}, f32[1]{0:T(128)}, f32[1]{0:T(128)}, /*index=5*/f32[1]{0:T(128)}, f32[1]{0:T(128)}, f32[1]{0:T(128)}) fusion(f32[8]{0:T(128)} %param.15), kind=kLoop, calls=%fused_computation.197 | loop fusion | bytes 64 | tf_op jit(solution)/shard_map/slice | solution.py:44
  18.3 0.9 convolution_bitcast_fusion
  19.9 3.4 %collective-permute-done.1 = f32[8,3,2048]{2,1,0:T(4,128)S(1)} collective-permute-done((f32[8,3,2048]{2,1,0:T(4,128)S(1)}, f32[8,3,2048]{2,1,0:T(4,128)S(1)}, u32[]{:S(2)}, u32[]{:S(2)}) %collective-permute-start.1) | collective-permute-done | bytes 196640 | tf_op jit(solution)/shard_map/ppermute | solution.py:21
  24.3 1.0 copy-done.1
  25.3 3.0 %fusion.7 = f32[8,34,2048]{2,1,0:T(8,128)S(1)} fusion(f32[8,36,2048]{2,1,0:T(8,128)S(1)} %pad_maximum_fusion, f32[8,2,2048]{2,1,0:T(2,128)S(1)} %slice.403, f32[8,32,2048]{2,1,0:T(8,128)S(1)} %copy-done, f32[8,2,2048]{2,1,0:T(2,128)S(1)} %slice.402, f32[8,1,2048]{2,1,0:T(1,128)S(1)} %slice.408, f32[8,32,2048]{2,1,0:T(8,128)S(1)} %copy-done.1, ...), kind=kLoop, calls=%fused_computation.13 | loop fusion | flops 8355840 | bytes 14353408 | tf_op jit(solution)/shard_map/jit(_where)/select_n | solution.py:101
  28.8 1.9 %fusion.15 = f32[8,32,2048]{2,1,0:T(8,128)S(1)} fusion(f32[8,32,2048]{2,1,0:T(8,128)S(1)} %copy-done.1, f32[8,34,2048]{2,1,0:T(8,128)S(1)} %fusion.7, f32[7,32,2048]{2,1,0:T(8,128)S(1)} %fusion.16, f32[8]{0:T(128)S(1)} %copy-done.9), kind=kLoop, calls=%fused_computation.24 | loop fusion | flops 5242880 | bytes 14942720 | tf_op jit(solution)/shard_map/add | solution.py:40
  30.7 5.2 %fusion.54 = f32[32,2048]{1,0:T(8,128)S(1)} fusion(f32[8,32,2048]{2,1,0:T(8,128)S(1)} %fusion.15, f32[]{:T(128)} %bitcast.8, f32[]{:T(128)} %bitcast.6, f32[]{:T(128)} %bitcast.5, f32[]{:T(128)} %bitcast.4, f32[]{:T(128)} %bitcast.3, f32[]{:T(128)} %bitcast.2, f32[]{:T(128)} %bitcast.1, f32[]{:T(128)} %bitcast), kind=kLoop, calls=%fused_computation.109 | loop fusion | flops 983040 | bytes 2359328 | tf_op jit(solution)/shard_map/add | solution.py:46
  35.9 2.5 %collective-permute-start.2 = (f32[2,2048]{1,0:T(2,128)S(1)}, f32[2,2048]{1,0:T(2,128)S(1)}, u32[]{:S(2)}, u32[]{:S(2)}) collective-permute-start(f32[2,2048]{1,0:T(2,128)S(1)} %get-tuple-element.33), channel_id=1, source_target_pairs={{0,1},{1,2},{2,3},{3,4},{4,5},{5,6},{6,7},{7,8},{8,9},{9,10},{10,1... | collective-permute-start | bytes 49160 | tf_op jit(solution)/shard_map/ppermute | solution.py:21
  38.4 1.3 collective-permute-start.3
  40.1 3.9 %collective-permute-done.3 = f32[2,2048]{1,0:T(2,128)S(1)} collective-permute-done((f32[2,2048]{1,0:T(2,128)S(1)}, f32[2,2048]{1,0:T(2,128)S(1)}, u32[]{:S(2)}, u32[]{:S(2)}) %collective-permute-start.3) | collective-permute-done | bytes 16416 | tf_op jit(solution)/shard_map/ppermute | solution.py:21
  45.3 1.2 pad_maximum_fusion.1
  46.5 5.4 %all-to-all-start = ((f32[4,2,36,516]{3,1,2,0:T(2,128)}), f32[4,2,36,516]{3,1,2,0:T(2,128)S(1)}, u32[]{:S(2)}, u32[]{:S(2)}) async-start(f32[4,2,36,516]{3,1,2,0:T(2,128)} %pad_maximum_fusion.1), calls=%async_computation | async-start | bytes 1474560 | tf_op jit(solution)/shard_map/all_to_all | solution.py:115
  52.1 3.9 %collective-permute-start.6 = (f32[2,134,3]{2,1,0:T(8,128)S(1)}, f32[2,134,3]{2,1,0:T(8,128)S(1)}, u32[]{:S(2)}, u32[]{:S(2)}) collective-permute-start(f32[2,134,3]{2,1,0:T(8,128)S(1)} %get-tuple-element.29), channel_id=1, source_target_pairs={{0,1},{1,2},{2,3},{4,5},{5,6},{6,7},{8,9},{9,10},{10,11},{12,13},{... | collective-permute-start | bytes 9656 | tf_op jit(solution)/shard_map/ppermute | solution.py:21
  56.0 1.5 %collective-permute-start.7 = (f32[2,134,3]{2,1,0:T(8,128)S(1)}, f32[2,134,3]{2,1,0:T(8,128)S(1)}, u32[]{:S(2)}, u32[]{:S(2)}) collective-permute-start(f32[2,134,3]{2,1,0:T(8,128)S(1)} %get-tuple-element.30), channel_id=1, source_target_pairs={{1,0},{2,1},{3,2},{5,4},{6,5},{7,6},{9,8},{10,9},{11,10},{13,12},{... | collective-permute-start | bytes 9656 | tf_op jit(solution)/shard_map/ppermute | solution.py:21
  57.5 9.2 %collective-permute-done.6 = f32[2,134,3]{2,1,0:T(8,128)S(1)} collective-permute-done((f32[2,134,3]{2,1,0:T(8,128)S(1)}, f32[2,134,3]{2,1,0:T(8,128)S(1)}, u32[]{:S(2)}, u32[]{:S(2)}) %collective-permute-start.6) | collective-permute-done | bytes 3248 | tf_op jit(solution)/shard_map/ppermute | solution.py:21
  67.1 4.3 %all-to-all-done = f32[4,2,36,516]{3,1,2,0:T(2,128)S(1)} async-done(((f32[4,2,36,516]{3,1,2,0:T(2,128)}), f32[4,2,36,516]{3,1,2,0:T(2,128)S(1)}, u32[]{:S(2)}, u32[]{:S(2)}) %all-to-all-start) | async-done | bytes 594464 | tf_op jit(solution)/shard_map/all_to_all | solution.py:115
  71.3 0.8 fusion.90
  73.5 0.9 fusion.23
  74.4 1.4 %subtract_bitcast_fusion = (f32[1,1,128,512]{3,2,1,0:T(8,128)S(1)}, f32[128,512]{1,0:T(8,128)}) fusion(f32[128,512]{1,0:T(8,128)S(1)} %copy-done.2, f32[130,514]{1,0:T(8,128)S(1)} %fusion.23, f32[134,518]{1,0:T(8,128)S(1)} %get-tuple-element.23, f32[132,516]{1,0:T(8,128)S(1)} %get-tuple-element.10), kind=kLoop, calls=%fused_computation.124 | loop fusion | flops 1441792 | bytes 3407872
  76.6 15.6 %copy.24 = f32[2,65536]{0,1:T(8,128)} copy(f32[2,65536]{1,0:T(2,128)S(1)} %pad_maximum_fusion.3) | data formatting | bytes 1048576 | tf_op jit(solution)/shard_map/stack | solution.py:185
  92.2 18.2 %gather_fusion = f32[2048,2]{1,0:T(8,128)} fusion(f32[2,65536]{0,1:T(8,128)} %copy.24, s32[2048]{0:T(1024)S(1)} %fusion.79), kind=kCustom, calls=%fused_computation | custom fusion | bytes 40960 | tf_op jit(solution)/shard_map/gather | solution.py:186
  110.4 6.8 %scatter_custom_fusion = f32[3,6144]{0,1:T(8,128)S(1)} fusion(s32[2048]{0:T(1024)S(1)} %bitcast.102, f32[]{:T(128)} %constant.34.clone.1, f32[2,2048]{0,1:T(8,128)} %bitcast.96, f32[]{:T(128)} %constant.45.clone.1), kind=kCustom, calls=%fused_computation.28 | custom fusion | bytes 90120 | tf_op jit(solution)/shard_map/scatter | solution.py:188
  117.2 1.5 %copy.25 = f32[3,32,192]{2,0,1:T(4,128)S(1)} copy(f32[3,32,192]{0,2,1:T(8,128)S(1)} %bitcast.89) | data formatting | bytes 147456 | tf_op jit(solution)/shard_map/all_to_all | solution.py:189
  118.7 15.4 %all_to_all.14 = f32[3,32,192]{2,0,1:T(4,128)S(1)} all-to-all(f32[3,32,192]{2,0,1:T(4,128)S(1)} %copy.25), channel_id=1, replica_groups=mesh['gx'=8,'gy'=4] {'gx','gy'}, dimensions={1} | all-to-all | bytes 147456 | tf_op jit(solution)/shard_map/all_to_all | solution.py:189
  134.9 1.1 add_select_fusion
  (75 shorter events, 8.0 us)
Async XLA Ops:
  0.6 22.7 %copy-start = (f32[8,32,2048]{2,1,0:T(8,128)S(1)}, f32[8,32,2048]{2,1,0:T(8,128)}, u32[]{:S(2)}) copy-start(f32[8,32,2048]{2,1,0:T(8,128)} %param.11) | copy-start | bytes 6291460
  0.6 19.0 %copy-start.5 = (s32[2048,1]{0,1:T(1,128)S(1)}, s32[2048,1]{0,1:T(1,128)}, u32[]{:S(2)}) copy-start(s32[2048,1]{0,1:T(1,128)} %param.19) | copy-start | bytes 24580
  0.7 19.2 %copy-start.7 = (s32[2048]{0:T(1024)S(1)}, s32[2048]{0:T(1024)}, u32[]{:S(2)}) copy-start(s32[2048]{0:T(1024)} %param.18) | copy-start | bytes 24580
  3.5 16.3 %collective-permute-start = (f32[8,3,2048]{2,1,0:T(4,128)S(1)}, f32[8,3,2048]{2,1,0:T(4,128)S(1)}, u32[]{:S(2)}, u32[]{:S(2)}) collective-permute-start(f32[8,3,2048]{2,1,0:T(4,128)S(1)} %pad_maximum_fusion.5), channel_id=1, source_target_pairs={{0,1},{1,2},{2,3},{3,4},{4,5},{5,6},{6,7},{7,8},{8,9},{9,10},{10,1... | collective-permute-start | bytes 589832 | tf_op jit(solution)/shard_map/ppermute | solution.py:21
  8.6 14.6 %collective-permute-start.1 = (f32[8,3,2048]{2,1,0:T(4,128)S(1)}, f32[8,3,2048]{2,1,0:T(4,128)S(1)}, u32[]{:S(2)}, u32[]{:S(2)}) collective-permute-start(f32[8,3,2048]{2,1,0:T(4,128)S(1)} %pad_maximum_fusion.6), channel_id=1, source_target_pairs={{1,0},{2,1},{3,2},{4,3},{5,4},{6,5},{7,6},{8,7},{9,8},{10,9},{11,1... | collective-permute-start | bytes 589832 | tf_op jit(solution)/shard_map/ppermute | solution.py:21
  10.7 41.2 %collective-permute-start.4 = (f32[2,3,512]{2,1,0:T(4,128)S(1)}, f32[2,3,512]{2,1,0:T(4,128)S(1)}, u32[]{:S(2)}, u32[]{:S(2)}) collective-permute-start(f32[2,3,512]{2,1,0:T(4,128)S(1)} %get-tuple-element.31), channel_id=1, source_target_pairs={{0,4},{4,8},{8,12},{12,16},{16,20},{20,24},{24,28},{1,5},{5,9},{9,... | collective-permute-start | bytes 36872 | tf_op jit(solution)/shard_map/ppermute | solution.py:21
  15.4 36.5 %collective-permute-start.5 = (f32[2,3,512]{2,1,0:T(4,128)S(1)}, f32[2,3,512]{2,1,0:T(4,128)S(1)}, u32[]{:S(2)}, u32[]{:S(2)}) collective-permute-start(f32[2,3,512]{2,1,0:T(4,128)S(1)} %get-tuple-element.32), channel_id=1, source_target_pairs={{4,0},{8,4},{12,8},{16,12},{20,16},{24,20},{28,24},{5,1},{9,5},{13... | collective-permute-start | bytes 36872 | tf_op jit(solution)/shard_map/ppermute | solution.py:21
  19.9 3.8 %copy-start.8 = (f32[7]{0:T(128)S(1)}, f32[7]{0:T(128)}, u32[]{:S(2)}) copy-start(f32[7]{0:T(128)} %param.14) | copy-start | bytes 88
  23.7 1.6 %copy-start.1 = (f32[8,32,2048]{2,1,0:T(8,128)S(1)}, f32[8,32,2048]{2,1,0:T(8,128)}, u32[]{:S(2)}) copy-start(f32[8,32,2048]{2,1,0:T(8,128)} %param.12) | copy-start | bytes 6291460
  23.8 1.6 %copy-start.9 = (f32[8]{0:T(128)S(1)}, f32[8]{0:T(128)}, u32[]{:S(2)}) copy-start(f32[8]{0:T(128)} %param.13) | copy-start | bytes 100
  35.9 4.2 %collective-permute-start.2 = (f32[2,2048]{1,0:T(2,128)S(1)}, f32[2,2048]{1,0:T(2,128)S(1)}, u32[]{:S(2)}, u32[]{:S(2)}) collective-permute-start(f32[2,2048]{1,0:T(2,128)S(1)} %get-tuple-element.33), channel_id=1, source_target_pairs={{0,1},{1,2},{2,3},{3,4},{4,5},{5,6},{6,7},{7,8},{8,9},{9,10},{10,1... | collective-permute-start | bytes 49160 | tf_op jit(solution)/shard_map/ppermute | solution.py:21
  38.4 5.6 %collective-permute-start.3 = (f32[2,2048]{1,0:T(2,128)S(1)}, f32[2,2048]{1,0:T(2,128)S(1)}, u32[]{:S(2)}, u32[]{:S(2)}) collective-permute-start(f32[2,2048]{1,0:T(2,128)S(1)} %get-tuple-element.34), channel_id=1, source_target_pairs={{1,0},{2,1},{3,2},{4,3},{5,4},{6,5},{7,6},{8,7},{9,8},{10,9},{11,1... | collective-permute-start | bytes 49160 | tf_op jit(solution)/shard_map/ppermute | solution.py:21
  44.2 7.7 %copy-start.2 = (f32[128,512]{1,0:T(8,128)S(1)}, f32[128,512]{1,0:T(8,128)}, u32[]{:S(2)}) copy-start(f32[128,512]{1,0:T(8,128)} %param.17) | copy-start | bytes 786436
  44.2 7.7 %copy-start.3 = (f32[128,512]{1,0:T(8,128)S(1)}, f32[128,512]{1,0:T(8,128)}, u32[]{:S(2)}) copy-start(f32[128,512]{1,0:T(8,128)} %param.16) | copy-start | bytes 786436
  46.5 24.8 %all-to-all-start = ((f32[4,2,36,516]{3,1,2,0:T(2,128)}), f32[4,2,36,516]{3,1,2,0:T(2,128)S(1)}, u32[]{:S(2)}, u32[]{:S(2)}) async-start(f32[4,2,36,516]{3,1,2,0:T(2,128)} %pad_maximum_fusion.1), calls=%async_computation | async-start | bytes 1474560 | tf_op jit(solution)/shard_map/all_to_all | solution.py:115
  52.1 14.6 %collective-permute-start.6 = (f32[2,134,3]{2,1,0:T(8,128)S(1)}, f32[2,134,3]{2,1,0:T(8,128)S(1)}, u32[]{:S(2)}, u32[]{:S(2)}) collective-permute-start(f32[2,134,3]{2,1,0:T(8,128)S(1)} %get-tuple-element.29), channel_id=1, source_target_pairs={{0,1},{1,2},{2,3},{4,5},{5,6},{6,7},{8,9},{9,10},{10,11},{12,13},{... | collective-permute-start | bytes 9656 | tf_op jit(solution)/shard_map/ppermute | solution.py:21
  56.0 10.7 %collective-permute-start.7 = (f32[2,134,3]{2,1,0:T(8,128)S(1)}, f32[2,134,3]{2,1,0:T(8,128)S(1)}, u32[]{:S(2)}, u32[]{:S(2)}) collective-permute-start(f32[2,134,3]{2,1,0:T(8,128)S(1)} %get-tuple-element.30), channel_id=1, source_target_pairs={{1,0},{2,1},{3,2},{5,4},{6,5},{7,6},{9,8},{10,9},{11,10},{13,12},{... | collective-permute-start | bytes 9656 | tf_op jit(solution)/shard_map/ppermute | solution.py:21
  117.2 17.7 %copy-start.4 = (f32[2,1,6144]{2,1,0:T(1,128)S(1)}, f32[2,1,6144]{2,1,0:T(1,128)}, u32[]{:S(2)}) copy-start(f32[2,1,6144]{2,1,0:T(1,128)} %param.20) | copy-start | bytes 147460
  117.2 17.7 %copy-start.6 = (f32[1,6144]{1,0:T(1,128)S(1)}, f32[1,6144]{1,0:T(1,128)}, u32[]{:S(2)}) copy-start(f32[1,6144]{1,0:T(1,128)} %param.21) | copy-start | bytes 73732
where the time goes:
time: 137 us
  local copies, waits for them, and re-layouts  51 us (37%)
  starting transfers between devices  26.7 us (19%)
  waiting for transfers between devices  20.8 us (15%)
  other arithmetic  20.7 us (15%)
  blocking collectives  15.4 us (11%)
    ppermute x8, starting transfers between devices, exchange(): return (lax.ppermute(last, axis, up), lax.ppermute(leading, axis, down))  21.4 us
    gather x1, local copies, waits for them, and re-layouts, body(): picked = fields[:, joint_cell]  18.2 us
    ppermute x8, waiting for transfers between devices, exchange(): return (lax.ppermute(last, axis, up), lax.ppermute(leading, axis, down))  16.5 us
    another operation x1, local copies, waits for them, and re-layouts, body(): fields = jnp.stack([(warp - warp_prev).reshape(-1), top.reshape(-1)])  15.6 us
    all_to_all x1, blocking collectives, body(): lax.all_to_all(outgoing, FLAT, split_axis=1, concat_axis=1, tiled=True)  15.4 us
    scatter x1, local copies, waits for them, and re-layouts, body(): jnp.zeros((3, devices * capacity), jnp.float32).at[:, slots].set(values)  6.81 us
    all_to_all x1, starting transfers between devices, relay(): recv = lax.all_to_all(send, 'gy', split_axis=0, concat_axis=0, tiled=True)  5.38 us
    add x1, other arithmetic, moment_of(): total = total + weighting[layer] * field[layer]  5.21 us
  transfers between devices with their start and end apart: 9, of which 4 were waited for; matrix products, arithmetic and copies ran while one was open for 14% of the time, Pallas kernels for 0%

commit v1 on v0

--- a/solution.py
+++ b/solution.py
@@ -186,7 +186,11 @@
     picked = fields[:, joint_cell]
     values = jnp.concatenate([picked, jnp.ones_like(picked[:1])], axis=0)
     outgoing = jnp.zeros((3, devices * capacity), jnp.float32).at[:, slots].set(values)
-    incoming = lax.all_to_all(outgoing, FLAT, split_axis=1, concat_axis=1, tiled=True)
+    t1 = lax.axis_size(FLAT)
+    right_arr = jnp.split(outgoing, t1, 1)
+    val2 = jnp.stack(right_arr)
+    row_out = lax.all_to_all(val2, FLAT, split_axis=0, concat_axis=0)
+    incoming = jnp.concatenate(row_out, 1)
     strain_next, resist_next = anand(joint_strain, joint_resist, incoming[:, None, :])
     return (warp, strain_next, resist_next)
 

time: 137 us -> 160 us (1.17)
  local copies, waits for them, and re-layouts: 51 us -> 72.9 us
    unnamed x22 -> x53, local copies, waits for them, and re-layouts: 1.59 us -> 21.6 us
    another operation x0 -> x2, local copies, waits for them, and re-layouts: none -> 3.31 us  [body(): val2 = jnp.stack(right_arr)]
  transfers between devices with their start and end apart: 9 -> 9, of which waited for: 4 -> 4; matrix products, arithmetic and copies ran while one was open for 14% -> 12% of each run, Pallas kernels for 0% -> 0%
where the time goes in v1:
time: 160 us; the launch traced here: 159 us
  local copies, waits for them, and re-layouts  72.9 us (46%)
  starting transfers between devices  27 us (17%)
  other arithmetic  21.3 us (13%)
  waiting for transfers between devices  20 us (12%)
  blocking collectives  15.7 us (10%)
    unnamed x53, local copies, waits for them, and re-layouts  21.6 us
    ppermute x8, starting transfers between devices, exchange(): return (lax.ppermute(last, axis, up), lax.ppermute(leading, axis, down))  21.4 us
    gather x1, local copies, waits for them, and re-layouts, body(): picked = fields[:, joint_cell]  18.2 us
    all_to_all x1, blocking collectives, body(): row_out = lax.all_to_all(val2, FLAT, split_axis=0, concat_axis=0)  15.7 us
    another operation x1, local copies, waits for them, and re-layouts, body(): fields = jnp.stack([(warp - warp_prev).reshape(-1), top.reshape(-1)])  15.6 us
    ppermute x8, waiting for transfers between devices, exchange(): return (lax.ppermute(last, axis, up), lax.ppermute(leading, axis, down))  15.6 us
    scatter x1, local copies, waits for them, and re-layouts, body(): jnp.zeros((3, devices * capacity), jnp.float32).at[:, slots].set(values)  6.81 us
    all_to_all x1, starting transfers between devices, relay(): recv = lax.all_to_all(send, 'gy', split_axis=0, concat_axis=0, tiled=True)  5.66 us
  transfers between devices with their start and end apart: 9, of which 4 were waited for; matrix products, arithmetic and copies ran while one was open for 12% of the time, Pallas kernels for 0%

profile of v1, /device:TPU:0, one launch (start us, length us, event | category | flops | bytes accessed | tf_op | source)
XLA Modules:
  0.0 159.2 jit_solution(2403248981146977094)
XLA Ops:
  0.7 1.4 fusion.120
  2.1 1.3 fusion.121
  3.5 5.0 %collective-permute-start = (f32[8,3,2048]{2,1,0:T(4,128)S(1)}, f32[8,3,2048]{2,1,0:T(4,128)S(1)}, u32[]{:S(2)}, u32[]{:S(2)}) collective-permute-start(f32[8,3,2048]{2,1,0:T(4,128)S(1)} %pad_maximum_fusion.5), channel_id=1, source_target_pairs={{0,1},{1,2},{2,3},{3,4},{4,5},{5,6},{6,7},{7,8},{8,9},{9,10},{10,1... | collective-permute-start | bytes 589832 | tf_op jit(solution)/shard_map/ppermute | solution.py:21
  8.6 1.3 collective-permute-start.1
  9.9 0.8 pad_maximum_fusion.14
  10.7 4.7 %collective-permute-start.4 = (f32[2,3,512]{2,1,0:T(4,128)S(1)}, f32[2,3,512]{2,1,0:T(4,128)S(1)}, u32[]{:S(2)}, u32[]{:S(2)}) collective-permute-start(f32[2,3,512]{2,1,0:T(4,128)S(1)} %get-tuple-element.31), channel_id=1, source_target_pairs={{0,4},{4,8},{8,12},{12,16},{16,20},{20,24},{24,28},{1,5},{5,9},{9,... | collective-permute-start | bytes 36872 | tf_op jit(solution)/shard_map/ppermute | solution.py:21
  15.4 1.3 collective-permute-start.5
  16.7 1.6 %fusion.126 = (f32[1]{0:T(128)}, f32[1]{0:T(128)}, f32[1]{0:T(128)}, f32[1]{0:T(128)}, f32[1]{0:T(128)}, /*index=5*/f32[1]{0:T(128)}, f32[1]{0:T(128)}, f32[1]{0:T(128)}) fusion(f32[8]{0:T(128)} %param.15), kind=kLoop, calls=%fused_computation.261 | loop fusion | bytes 64 | tf_op jit(solution)/shard_map/slice | solution.py:44
  18.3 0.9 convolution_bitcast_fusion
  19.6 0.9 select_reduce_fusion
  20.6 2.7 %collective-permute-done.1 = f32[8,3,2048]{2,1,0:T(4,128)S(1)} collective-permute-done((f32[8,3,2048]{2,1,0:T(4,128)S(1)}, f32[8,3,2048]{2,1,0:T(4,128)S(1)}, u32[]{:S(2)}, u32[]{:S(2)}) %collective-permute-start.1) | collective-permute-done | bytes 196640 | tf_op jit(solution)/shard_map/ppermute | solution.py:21
  24.3 1.0 copy-done.1
  25.3 3.0 %fusion.7 = f32[8,34,2048]{2,1,0:T(8,128)S(1)} fusion(f32[8,36,2048]{2,1,0:T(8,128)S(1)} %pad_maximum_fusion, f32[8,2,2048]{2,1,0:T(2,128)S(1)} %slice.391, f32[8,32,2048]{2,1,0:T(8,128)S(1)} %copy-done, f32[8,2,2048]{2,1,0:T(2,128)S(1)} %slice.390, f32[8,1,2048]{2,1,0:T(1,128)S(1)} %slice.396, f32[8,32,2048]{2,1,0:T(8,128)S(1)} %copy-done.1, ...), kind=kLoop, calls=%fused_computation.13 | loop fusion | flops 8355840 | bytes 14353408 | tf_op jit(solution)/shard_map/jit(_where)/select_n | solution.py:101
  28.8 1.9 %fusion.15 = f32[8,32,2048]{2,1,0:T(8,128)S(1)} fusion(f32[8,32,2048]{2,1,0:T(8,128)S(1)} %copy-done.1, f32[8,34,2048]{2,1,0:T(8,128)S(1)} %fusion.7, f32[7,32,2048]{2,1,0:T(8,128)S(1)} %fusion.16, f32[8]{0:T(128)S(1)} %copy-done.9), kind=kLoop, calls=%fused_computation.24 | loop fusion | flops 5242880 | bytes 14942720 | tf_op jit(solution)/shard_map/add | solution.py:40
  30.7 5.2 %fusion.54 = f32[32,2048]{1,0:T(8,128)S(1)} fusion(f32[8,32,2048]{2,1,0:T(8,128)S(1)} %fusion.15, f32[]{:T(128)} %bitcast.8, f32[]{:T(128)} %bitcast.6, f32[]{:T(128)} %bitcast.5, f32[]{:T(128)} %bitcast.4, f32[]{:T(128)} %bitcast.3, f32[]{:T(128)} %bitcast.2, f32[]{:T(128)} %bitcast.1, f32[]{:T(128)} %bitcast), kind=kLoop, calls=%fused_computation.109 | loop fusion | flops 983040 | bytes 2359328 | tf_op jit(solution)/shard_map/add | solution.py:46
  35.9 2.5 %collective-permute-start.2 = (f32[2,2048]{1,0:T(2,128)S(1)}, f32[2,2048]{1,0:T(2,128)S(1)}, u32[]{:S(2)}, u32[]{:S(2)}) collective-permute-start(f32[2,2048]{1,0:T(2,128)S(1)} %get-tuple-element.33), channel_id=1, source_target_pairs={{0,1},{1,2},{2,3},{3,4},{4,5},{5,6},{6,7},{7,8},{8,9},{9,10},{10,1... | collective-permute-start | bytes 49160 | tf_op jit(solution)/shard_map/ppermute | solution.py:21
  38.4 1.3 collective-permute-start.3
  40.2 3.9 %collective-permute-done.3 = f32[2,2048]{1,0:T(2,128)S(1)} collective-permute-done((f32[2,2048]{1,0:T(2,128)S(1)}, f32[2,2048]{1,0:T(2,128)S(1)}, u32[]{:S(2)}, u32[]{:S(2)}) %collective-permute-start.3) | collective-permute-done | bytes 16416 | tf_op jit(solution)/shard_map/ppermute | solution.py:21
  45.3 1.2 pad_maximum_fusion.1
  46.5 5.7 %all-to-all-start = ((f32[4,2,36,516]{3,1,2,0:T(2,128)}), f32[4,2,36,516]{3,1,2,0:T(2,128)S(1)}, u32[]{:S(2)}, u32[]{:S(2)}) async-start(f32[4,2,36,516]{3,1,2,0:T(2,128)} %pad_maximum_fusion.1), calls=%async_computation | async-start | bytes 1474560 | tf_op jit(solution)/shard_map/all_to_all | solution.py:115
  52.3 3.9 %collective-permute-start.6 = (f32[2,134,3]{2,1,0:T(8,128)S(1)}, f32[2,134,3]{2,1,0:T(8,128)S(1)}, u32[]{:S(2)}, u32[]{:S(2)}) collective-permute-start(f32[2,134,3]{2,1,0:T(8,128)S(1)} %get-tuple-element.29), channel_id=1, source_target_pairs={{0,1},{1,2},{2,3},{4,5},{5,6},{6,7},{8,9},{9,10},{10,11},{12,13},{... | collective-permute-start | bytes 9656 | tf_op jit(solution)/shard_map/ppermute | solution.py:21
  56.3 1.5 collective-permute-start.7
  57.8 9.0 %collective-permute-done.6 = f32[2,134,3]{2,1,0:T(8,128)S(1)} collective-permute-done((f32[2,134,3]{2,1,0:T(8,128)S(1)}, f32[2,134,3]{2,1,0:T(8,128)S(1)}, u32[]{:S(2)}, u32[]{:S(2)}) %collective-permute-start.6) | collective-permute-done | bytes 3248 | tf_op jit(solution)/shard_map/ppermute | solution.py:21
  67.2 4.4 %all-to-all-done = f32[4,2,36,516]{3,1,2,0:T(2,128)S(1)} async-done(((f32[4,2,36,516]{3,1,2,0:T(2,128)}), f32[4,2,36,516]{3,1,2,0:T(2,128)S(1)}, u32[]{:S(2)}, u32[]{:S(2)}) %all-to-all-start) | async-done | bytes 594464 | tf_op jit(solution)/shard_map/all_to_all | solution.py:115
  73.8 0.9 fusion.23
  74.7 1.4 subtract_bitcast_fusion
  76.9 15.6 %copy.64 = f32[2,65536]{0,1:T(8,128)} copy(f32[2,65536]{1,0:T(2,128)S(1)} %pad_maximum_fusion.3) | data formatting | bytes 1048576 | tf_op jit(solution)/shard_map/stack | solution.py:185
  92.5 18.2 %gather_fusion = f32[2048,2]{1,0:T(8,128)} fusion(f32[2,65536]{0,1:T(8,128)} %copy.64, s32[2048]{0:T(1024)S(1)} %fusion.111), kind=kCustom, calls=%fused_computation | custom fusion | bytes 40960 | tf_op jit(solution)/shard_map/gather | solution.py:186
  110.7 6.8 %scatter_custom_fusion = f32[3,6144]{0,1:T(8,128)S(1)} fusion(s32[2048]{0:T(1024)S(1)} %bitcast.231, f32[]{:T(128)} %constant.34.clone.1, f32[2,2048]{0,1:T(8,128)} %bitcast.223, f32[]{:T(128)} %constant.45.clone.1), kind=kCustom, calls=%fused_computation.28 | custom fusion | bytes 90120 | tf_op jit(solution)/shard_map/scatter | solution.py:188
  138.2 2.7 %copy.65 = f32[32,3,192]{2,1,0:T(4,128)S(1)} copy(f32[32,3,192]{1,2,0:T(8,128)} %fusion.68) | data formatting | bytes 147456 | tf_op jit(solution)/shard_map/stack | solution.py:191
  140.8 15.7 %all_to_all.10 = f32[32,3,192]{2,1,0:T(4,128)S(1)} all-to-all(f32[32,3,192]{2,1,0:T(4,128)S(1)} %copy.65), channel_id=1, replica_groups=mesh['gx'=8,'gy'=4] {'gx','gy'}, dimensions={0} | all-to-all | bytes 147456 | tf_op jit(solution)/shard_map/all_to_all | solution.py:192
  157.3 1.1 add_select_fusion
  (107 shorter events, 29.3 us)
Async XLA Ops:
  0.6 22.7 %copy-start = (f32[8,32,2048]{2,1,0:T(8,128)S(1)}, f32[8,32,2048]{2,1,0:T(8,128)}, u32[]{:S(2)}) copy-start(f32[8,32,2048]{2,1,0:T(8,128)} %param.11) | copy-start | bytes 6291460
  0.6 19.9 %copy-start.5 = (s32[2048,1]{0,1:T(1,128)S(1)}, s32[2048,1]{0,1:T(1,128)}, u32[]{:S(2)}) copy-start(s32[2048,1]{0,1:T(1,128)} %param.19) | copy-start | bytes 24580
  0.7 19.9 %copy-start.7 = (s32[2048]{0:T(1024)S(1)}, s32[2048]{0:T(1024)}, u32[]{:S(2)}) copy-start(s32[2048]{0:T(1024)} %param.18) | copy-start | bytes 24580
  3.5 17.0 %collective-permute-start = (f32[8,3,2048]{2,1,0:T(4,128)S(1)}, f32[8,3,2048]{2,1,0:T(4,128)S(1)}, u32[]{:S(2)}, u32[]{:S(2)}) collective-permute-start(f32[8,3,2048]{2,1,0:T(4,128)S(1)} %pad_maximum_fusion.5), channel_id=1, source_target_pairs={{0,1},{1,2},{2,3},{3,4},{4,5},{5,6},{6,7},{7,8},{8,9},{9,10},{10,1... | collective-permute-start | bytes 589832 | tf_op jit(solution)/shard_map/ppermute | solution.py:21
  8.6 14.6 %collective-permute-start.1 = (f32[8,3,2048]{2,1,0:T(4,128)S(1)}, f32[8,3,2048]{2,1,0:T(4,128)S(1)}, u32[]{:S(2)}, u32[]{:S(2)}) collective-permute-start(f32[8,3,2048]{2,1,0:T(4,128)S(1)} %pad_maximum_fusion.6), channel_id=1, source_target_pairs={{1,0},{2,1},{3,2},{4,3},{5,4},{6,5},{7,6},{8,7},{9,8},{10,9},{11,1... | collective-permute-start | bytes 589832 | tf_op jit(solution)/shard_map/ppermute | solution.py:21
  10.7 41.5 %collective-permute-start.4 = (f32[2,3,512]{2,1,0:T(4,128)S(1)}, f32[2,3,512]{2,1,0:T(4,128)S(1)}, u32[]{:S(2)}, u32[]{:S(2)}) collective-permute-start(f32[2,3,512]{2,1,0:T(4,128)S(1)} %get-tuple-element.31), channel_id=1, source_target_pairs={{0,4},{4,8},{8,12},{12,16},{16,20},{20,24},{24,28},{1,5},{5,9},{9,... | collective-permute-start | bytes 36872 | tf_op jit(solution)/shard_map/ppermute | solution.py:21
  15.4 36.8 %collective-permute-start.5 = (f32[2,3,512]{2,1,0:T(4,128)S(1)}, f32[2,3,512]{2,1,0:T(4,128)S(1)}, u32[]{:S(2)}, u32[]{:S(2)}) collective-permute-start(f32[2,3,512]{2,1,0:T(4,128)S(1)} %get-tuple-element.32), channel_id=1, source_target_pairs={{4,0},{8,4},{12,8},{16,12},{20,16},{24,20},{28,24},{5,1},{9,5},{13... | collective-permute-start | bytes 36872 | tf_op jit(solution)/shard_map/ppermute | solution.py:21
  18.3 5.4 %copy-start.8 = (f32[7]{0:T(128)S(1)}, f32[7]{0:T(128)}, u32[]{:S(2)}) copy-start(f32[7]{0:T(128)} %param.14) | copy-start | bytes 88
  23.7 1.6 %copy-start.1 = (f32[8,32,2048]{2,1,0:T(8,128)S(1)}, f32[8,32,2048]{2,1,0:T(8,128)}, u32[]{:S(2)}) copy-start(f32[8,32,2048]{2,1,0:T(8,128)} %param.12) | copy-start | bytes 6291460
  23.8 1.6 copy-start.9
  35.9 4.2 %collective-permute-start.2 = (f32[2,2048]{1,0:T(2,128)S(1)}, f32[2,2048]{1,0:T(2,128)S(1)}, u32[]{:S(2)}, u32[]{:S(2)}) collective-permute-start(f32[2,2048]{1,0:T(2,128)S(1)} %get-tuple-element.33), channel_id=1, source_target_pairs={{0,1},{1,2},{2,3},{3,4},{4,5},{5,6},{6,7},{7,8},{8,9},{9,10},{10,1... | collective-permute-start | bytes 49160 | tf_op jit(solution)/shard_map/ppermute | solution.py:21
  38.4 5.6 %collective-permute-start.3 = (f32[2,2048]{1,0:T(2,128)S(1)}, f32[2,2048]{1,0:T(2,128)S(1)}, u32[]{:S(2)}, u32[]{:S(2)}) collective-permute-start(f32[2,2048]{1,0:T(2,128)S(1)} %get-tuple-element.34), channel_id=1, source_target_pairs={{1,0},{2,1},{3,2},{4,3},{5,4},{6,5},{7,6},{8,7},{9,8},{10,9},{11,1... | collective-permute-start | bytes 49160 | tf_op jit(solution)/shard_map/ppermute | solution.py:21
  39.9 12.3 %copy-start.2 = (f32[128,512]{1,0:T(8,128)S(1)}, f32[128,512]{1,0:T(8,128)}, u32[]{:S(2)}) copy-start(f32[128,512]{1,0:T(8,128)} %param.17) | copy-start | bytes 786436
  39.9 12.3 %copy-start.3 = (f32[128,512]{1,0:T(8,128)S(1)}, f32[128,512]{1,0:T(8,128)}, u32[]{:S(2)}) copy-start(f32[128,512]{1,0:T(8,128)} %param.16) | copy-start | bytes 786436
  46.5 25.1 %all-to-all-start = ((f32[4,2,36,516]{3,1,2,0:T(2,128)}), f32[4,2,36,516]{3,1,2,0:T(2,128)S(1)}, u32[]{:S(2)}, u32[]{:S(2)}) async-start(f32[4,2,36,516]{3,1,2,0:T(2,128)} %pad_maximum_fusion.1), calls=%async_computation | async-start | bytes 1474560 | tf_op jit(solution)/shard_map/all_to_all | solution.py:115
  52.3 14.5 %collective-permute-start.6 = (f32[2,134,3]{2,1,0:T(8,128)S(1)}, f32[2,134,3]{2,1,0:T(8,128)S(1)}, u32[]{:S(2)}, u32[]{:S(2)}) collective-permute-start(f32[2,134,3]{2,1,0:T(8,128)S(1)} %get-tuple-element.29), channel_id=1, source_target_pairs={{0,1},{1,2},{2,3},{4,5},{5,6},{6,7},{8,9},{9,10},{10,11},{12,13},{... | collective-permute-start | bytes 9656 | tf_op jit(solution)/shard_map/ppermute | solution.py:21
  56.3 10.5 %collective-permute-start.7 = (f32[2,134,3]{2,1,0:T(8,128)S(1)}, f32[2,134,3]{2,1,0:T(8,128)S(1)}, u32[]{:S(2)}, u32[]{:S(2)}) collective-permute-start(f32[2,134,3]{2,1,0:T(8,128)S(1)} %get-tuple-element.30), channel_id=1, source_target_pairs={{1,0},{2,1},{3,2},{5,4},{6,5},{7,6},{9,8},{10,9},{11,10},{13,12},{... | collective-permute-start | bytes 9656 | tf_op jit(solution)/shard_map/ppermute | solution.py:21
  130.4 26.9 %copy-start.4 = (f32[2,1,6144]{2,1,0:T(1,128)S(1)}, f32[2,1,6144]{2,1,0:T(1,128)}, u32[]{:S(2)}) copy-start(f32[2,1,6144]{2,1,0:T(1,128)} %param.20) | copy-start | bytes 147460
  130.4 26.9 %copy-start.6 = (f32[1,6144]{1,0:T(1,128)S(1)}, f32[1,6144]{1,0:T(1,128)}, u32[]{:S(2)}) copy-start(f32[1,6144]{1,0:T(1,128)} %param.21) | copy-start | bytes 73732
